TPU v7x, 512 devices: a whole 4x8x8 slice. The times are simulated.
512 devices in a mesh: seq: 128 (over z, y_hi, x, core), head: 4 (over y_lo).
Axes of the slice: x: 4, y: 8 (y_hi: 2, y_lo: 4; y = y_hi * 4 + y_lo), z: 8, core: 2. Of those that a mesh axis runs over, the one named last changes fastest.
Arguments:
- query_rows: bfloat16 [32768, 8, 128], P('seq', 'head'), may hold values from -20 to 20
- key_rows: bfloat16 [32768, 8, 128], P('seq', 'head'), may hold values from -20 to 20
- value_rows: bfloat16 [32768, 8, 128], P('seq', 'head'), may hold values from -6 to 6
- cotangent: bfloat16 [32768, 8, 128], P('seq', 'head'), may hold values from -6 to 6
- norm_gain: float32 [8, 128], P('head'), may hold values from 0.5 to 2
- offsets: int32 [8], P('head'), may hold values from 0 to 31, as said below
Outputs:
- query_grad: bfloat16 [32768, 8, 128], P('seq', 'head')
- key_grad: bfloat16 [32768, 8, 128], P('seq', 'head')
- value_grad: bfloat16 [32768, 8, 128], P('seq', 'head')
Inputs may be any that keep to these rules, and one draw needn't show every extreme that they name: The heads' offsets are distinct.
All inputs are finite; a program needn't handle non-finite values.
Results may differ from a plain program's by a relative error of at most 0.018.
Values may be sent and summed in bfloat16 or wider, within the bound.
No kernel may reach another device: no remote copies, remote signals or barrier semaphores. Data moves between devices by JAX's collectives and lax.ppermute only.
A program may use at most 128 MiB of HBM per device.

v0:
```python
import numpy as np
import jax
import jax.numpy as jnp
from jax import lax
from jax.sharding import PartitionSpec as P

RATE2 = 4
RATE3 = 16
RATE4 = 32
RATES = (1, RATE2, RATE3, RATE4)
neg_fill = -1e30
epsilon = 1e-05
lane = 128


def pick_rows(source, wanted, stride):
    row_count = source.shape[0] // stride
    shaped = source.reshape((row_count, stride) + source.shape[1:])
    trailing = (1,) * (source.ndim - 2)
    target = wanted.reshape((1, 1, -1) + trailing)
    column = jnp.arange(stride, dtype=jnp.int32).reshape((1, stride, 1) + trailing)
    zeroed = jnp.where(column == target, shaped, jnp.zeros((), source.dtype))
    return jnp.sum(zeroed, axis=1, dtype=source.dtype)


def put_rows(compact, wanted, stride, filler):
    trailing = (1,) * (compact.ndim - 2)
    target = wanted.reshape((1, 1, -1) + trailing)
    column = jnp.arange(stride, dtype=jnp.int32).reshape((1, stride, 1) + trailing)
    spread = jnp.where(column == target, compact[:, None], jnp.asarray(filler, compact.dtype))
    return spread.reshape((compact.shape[0] * stride,) + compact.shape[1:])


def exchange_order(count):
    bits = [1 << bit for bit in range(max(0, (count - 1).bit_length()))]
    order = []
    for first in range(0, len(bits), 2):
        order.extend(reversed(bits[first : first + 2]))
    return order


def spread(order, slots):
    table = np.zeros(slots, np.int32)
    for slot in range(slots):
        for bit, offset in enumerate(order):
            if slot >> bit & 1:
                table[slot] ^= offset
    return table


def extend(parts, spans, order, toward):
    count = lax.axis_size("seq")
    live = sorted(range(len(parts)), key=lambda index: -spans[index])
    sizes = [part.shape[0] for part in parts]
    state = jnp.concatenate([parts[index] for index in live], axis=0)[None]
    finished = {}
    for offset in order + [None]:
        while live and spans[live[-1]] <= state.shape[0]:
            index = live.pop()
            start = sum((sizes[other] for other in live))
            finished[index] = state[:, start : start + sizes[index]]
            state = state[:, :start]
        if not live:
            break
        pairs = [(source, source ^ offset) for source in range(count)]
        if all((spans[index] <= 2 * state.shape[0] for index in live)):
            pairs = [pair for pair in pairs if (pair[1] > pair[0]) == (toward > 0)]
        moved = lax.ppermute(state, "seq", pairs)
        state = jnp.concatenate([state, moved], axis=0)
    return [finished[index] for index in range(len(parts))]


def split_exact(value):
    high = lax.reduce_precision(value, exponent_bits=8, mantissa_bits=7)
    rest = value - high
    middle = lax.reduce_precision(rest, exponent_bits=8, mantissa_bits=7)
    low = rest - middle
    return jnp.stack([high, middle, low]).astype(jnp.bfloat16)


def stats_rows(rows, heads_dev):
    return -(-(rows * heads_dev * 6) // (16 * lane)) * 16


def pack_stats(lse_sel, delta_sel):
    rows, heads_dev = lse_sel.shape
    coded = split_exact(jnp.stack([lse_sel.T, delta_sel.T])).reshape(-1)
    padded = stats_rows(rows, heads_dev) * lane
    coded = jnp.pad(coded, (0, padded - coded.shape[0]))
    return coded.reshape(padded // lane, lane)


def unpack_stats(coded, slots, rows, heads_dev):
    width = 2 * heads_dev * rows
    parts = coded.reshape(slots, -1)[:, : 3 * width].reshape(slots, 3, width)
    parts = parts.astype(jnp.float32)
    values = parts[:, 0] + parts[:, 1] + parts[:, 2]
    values = values.reshape(slots, 2, heads_dev, rows).transpose(1, 2, 0, 3)
    values = values.reshape(2, heads_dev, slots * rows)
    return (values[0], values[1])


def shards(query_rows, key_rows, value_rows, cotangent, norm_gain, offsets):
    tok_dev, heads_dev, head_size = query_rows.shape
    seq_count = lax.axis_size("seq")
    device = lax.axis_index("seq")
    group_rows = tok_dev * seq_count // RATE4
    score_scale = head_size ** (-0.5)
    features = heads_dev * head_size * lax.axis_size("head")
    levels = []
    for stride in RATES:
        span = max(1, stride * group_rows // tok_dev)
        rows = tok_dev // stride
        wanted = offsets % stride
        levels.append(
            dict(
                stride=stride,
                span=span,
                rows=rows,
                wanted=wanted,
                spot=device % span,
                key_sel=pick_rows(key_rows, wanted, stride),
                value_sel=pick_rows(value_rows, wanted, stride),
                query_sel=pick_rows(query_rows, wanted, stride),
            )
        )
    spans = [level["span"] for level in levels]
    order = exchange_order(seq_count)
    for level in levels:
        level["owner"] = level["spot"] ^ jnp.asarray(spread(order, level["span"]))
    key_sets = extend(
        [
            jnp.concatenate(
                [level["key_sel"].reshape(-1, lane), level["value_sel"].reshape(-1, lane)], axis=0
            )
            for level in levels
        ],
        spans,
        order,
        1,
    )
    query_sets = extend(
        [level["query_sel"].reshape(-1, lane) for level in levels], spans, order, -1
    )
    lse_total = jnp.full((tok_dev, heads_dev), neg_fill, jnp.float32)
    for level, key_set in zip(levels, key_sets):
        span, rows = (level["span"], level["rows"])
        paired = key_set.reshape(span, 2, rows, heads_dev, head_size)
        keys = paired[:, 0].reshape(span * rows, heads_dev, head_size)
        level["key_all"] = keys
        level["value_all"] = paired[:, 1].reshape(span * rows, heads_dev, head_size)
        raw = (
            jnp.einsum("qhd,khd->hqk", level["query_sel"], keys, preferred_element_type=jnp.float32)
            * score_scale
        )
        key_at = (
            level["owner"][:, None] * rows + jnp.arange(rows, dtype=jnp.int32)[None, :]
        ).reshape(1, span * rows)
        query_at = (level["spot"] * rows + jnp.arange(rows, dtype=jnp.int32))[:, None]
        linked = key_at <= query_at
        scores = jnp.where(linked[None], raw, neg_fill)
        row_peak = jnp.max(scores, axis=2)
        level_lse = row_peak + jnp.log(jnp.sum(jnp.exp(scores - row_peak[:, :, None]), axis=2))
        level["scores"] = scores
        lse_total = jnp.logaddexp(
            lse_total, put_rows(level_lse.T, level["wanted"], level["stride"], neg_fill)
        )
    attended = jnp.zeros((tok_dev, heads_dev, head_size), jnp.float32)
    for level in levels:
        lse_sel = pick_rows(lse_total, level["wanted"], level["stride"])
        weights = jnp.exp(level["scores"] - lse_sel.T[:, :, None])
        level["lse_sel"] = lse_sel
        level["weights"] = weights
        out_sel = jnp.einsum(
            "hqk,khd->qhd",
            weights.astype(jnp.bfloat16),
            level["value_all"],
            preferred_element_type=jnp.float32,
        )
        attended = attended + put_rows(out_sel, level["wanted"], level["stride"], 0.0)
    grad_in = cotangent.astype(jnp.float32) * norm_gain[None]
    sums = lax.psum(
        jnp.stack(
            [
                jnp.sum(attended, axis=(1, 2)),
                jnp.sum(attended * attended, axis=(1, 2)),
                jnp.sum(grad_in, axis=(1, 2)),
                jnp.sum(grad_in * attended, axis=(1, 2)),
            ]
        ),
        "head",
    )
    centre = sums[0] / features
    variance = sums[1] / features - centre * centre
    inverse = lax.rsqrt(variance + epsilon)
    first_mean = sums[2] / features
    second_mean = inverse * (sums[3] / features - centre * first_mean)
    normed = (attended - centre[:, None, None]) * inverse[:, None, None]
    d_attended = (
        inverse[:, None, None]
        * (grad_in - first_mean[:, None, None] - normed * second_mean[:, None, None])
    ).astype(jnp.bfloat16)
    row_delta = jnp.sum(d_attended.astype(jnp.float32) * attended, axis=2)
    query_grad = jnp.zeros((tok_dev, heads_dev, head_size), jnp.float32)
    back_sets = []
    for level in levels:
        dout_sel = pick_rows(d_attended, level["wanted"], level["stride"])
        delta_sel = pick_rows(row_delta, level["wanted"], level["stride"])
        back_sets.append(
            jnp.concatenate(
                [dout_sel.reshape(-1, lane), pack_stats(level["lse_sel"], delta_sel)], axis=0
            )
        )
        weight_grad = jnp.einsum(
            "qhd,khd->hqk", dout_sel, level["value_all"], preferred_element_type=jnp.float32
        )
        score_grad = (level["weights"] * (weight_grad - delta_sel.T[:, :, None])).astype(
            jnp.bfloat16
        )
        grad_sel = jnp.einsum(
            "hqk,khd->qhd", score_grad, level["key_all"], preferred_element_type=jnp.float32
        )
        query_grad = query_grad + put_rows(
            grad_sel * score_scale, level["wanted"], level["stride"], 0.0
        )
    back_sets = extend(back_sets, spans, order, -1)
    key_grad = jnp.zeros((tok_dev, heads_dev, head_size), jnp.float32)
    value_grad = jnp.zeros((tok_dev, heads_dev, head_size), jnp.float32)
    for level, query_set, back_set in zip(levels, query_sets, back_sets):
        span, rows = (level["span"], level["rows"])
        queries = query_set.reshape(span * rows, heads_dev, head_size)
        back_slots = back_set.reshape(span, -1, lane)
        dout_all = back_slots[:, : rows * heads_dev].reshape(span * rows, heads_dev, head_size)
        lse_all, delta_all = unpack_stats(back_slots[:, rows * heads_dev :], span, rows, heads_dev)
        raw = (
            jnp.einsum(
                "qhd,khd->hqk", queries, level["key_sel"], preferred_element_type=jnp.float32
            )
            * score_scale
        )
        query_at = (
            level["owner"][:, None] * rows + jnp.arange(rows, dtype=jnp.int32)[None, :]
        ).reshape(span * rows, 1)
        key_at = (level["spot"] * rows + jnp.arange(rows, dtype=jnp.int32))[None, :]
        linked = query_at >= key_at
        scores = jnp.where(linked[None], raw, neg_fill)
        weights = jnp.exp(scores - lse_all[:, :, None])
        value_grad_sel = jnp.einsum(
            "hqk,qhd->khd",
            weights.astype(jnp.bfloat16),
            dout_all,
            preferred_element_type=jnp.float32,
        )
        weight_grad = jnp.einsum(
            "qhd,khd->hqk", dout_all, level["value_sel"], preferred_element_type=jnp.float32
        )
        score_grad = (weights * (weight_grad - delta_all[:, :, None])).astype(jnp.bfloat16)
        key_grad_sel = jnp.einsum(
            "hqk,qhd->khd", score_grad, queries, preferred_element_type=jnp.float32
        )
        key_grad = key_grad + put_rows(
            key_grad_sel * score_scale, level["wanted"], level["stride"], 0.0
        )
        value_grad = value_grad + put_rows(value_grad_sel, level["wanted"], level["stride"], 0.0)
    return (
        query_grad.astype(jnp.bfloat16),
        key_grad.astype(jnp.bfloat16),
        value_grad.astype(jnp.bfloat16),
    )


def solution(mesh):
    placed = (
        P("seq", "head", None),
        P("seq", "head", None),
        P("seq", "head", None),
        P("seq", "head", None),
        P("head", None),
        P("head"),
    )
    return jax.shard_map(
        shards,
        mesh=mesh,
        in_specs=placed,
        out_specs=(P("seq", "head", None), P("seq", "head", None), P("seq", "head", None)),
        check_vma=False,
    )
```

profile of v0, /device:TPU:74, one launch (start us, length us, event | category | flops | bytes accessed | tf_op | source)
XLA Modules:
  0.0 368.6 jit_solution(18264421656202876044)
XLA Ops:
  8.0 2.4 collective-permute-start
  10.6 3.5 collective-permute-start.7
  19.5 4.2 %collective-permute-done.7 = bf16[1,688,128]{2,1,0:T(8,128)(2,1)S(1)} collective-permute-done((bf16[1,688,128]{2,1,0:T(8,128)(2,1)S(1)}, bf16[1,688,128]{2,1,0:T(8,128)(2,1)S(1)}, u32[]{:S(2)}, u32[]{:S(2)}) %collective-permute-start.7) | collective-permute-done | bytes 176160 | tf_op jit(solution)/shard_map/ppermute | solution.py:68
  23.7 1.9 collective-permute-start.8
  26.6 2.4 collective-permute-start.1
  29.7 6.8 %collective-permute-start.11 = (bf16[4,176,128]{2,1,0:T(8,128)(2,1)S(1)}, bf16[4,176,128]{2,1,0:T(8,128)(2,1)S(1)}, u32[]{:S(2)}, u32[]{:S(2)}) collective-permute-start(bf16[4,176,128]{2,1,0:T(8,128)(2,1)S(1)} %pad_maximum_fusion.31), channel_id=1, source_target_pairs={{0,32},{4,36},{8,40},{12,44},{16,48},{20,52},{24,56},{28,60},{32,0... | collective-permute-start | bytes 540680 | tf_op jit(solution)/shard_map/ppermute | solution.py:68
  42.2 2.4 collective-permute-done.11
  44.7 4.0 %collective-permute-start.12 = (bf16[8,176,128]{2,1,0:T(8,128)(2,1)S(1)}, bf16[8,176,128]{2,1,0:T(8,128)(2,1)S(1)}, u32[]{:S(2)}, u32[]{:S(2)}) collective-permute-start(bf16[8,176,128]{2,1,0:T(8,128)(2,1)S(1)} %pad_maximum_fusion.24), channel_id=1, source_target_pairs={{0,16},{4,20},{8,24},{12,28},{16,0},{20,4},{24,8},{28,12},{32,48},... | collective-permute-start | bytes 1081352 | tf_op jit(solution)/shard_map/ppermute | solution.py:68
  49.0 7.0 %collective-permute-start.2 = (bf16[4,352,128]{2,1,0:T(8,128)(2,1)S(1)}, bf16[4,352,128]{2,1,0:T(8,128)(2,1)S(1)}, u32[]{:S(2)}, u32[]{:S(2)}) collective-permute-start(bf16[4,352,128]{2,1,0:T(8,128)(2,1)S(1)} %pad_maximum_fusion.23), channel_id=1, source_target_pairs={{0,32},{4,36},{8,40},{12,44},{16,48},{20,52},{24,56},{28,60},{32,0... | collective-permute-start | bytes 1081352 | tf_op jit(solution)/shard_map/ppermute | solution.py:68
  58.4 6.1 %collective-permute-start.15 = (bf16[16,48,128]{2,1,0:T(8,128)(2,1)S(1)}, bf16[16,48,128]{2,1,0:T(8,128)(2,1)S(1)}, u32[]{:S(2)}, u32[]{:S(2)}) collective-permute-start(bf16[16,48,128]{2,1,0:T(8,128)(2,1)S(1)} %pad_maximum_fusion.30), channel_id=1, source_target_pairs={{0,128},{4,132},{8,136},{12,140},{16,144},{20,148},{24,152},{28,15... | collective-permute-start | bytes 589832 | tf_op jit(solution)/shard_map/ppermute | solution.py:68
  66.5 3.7 %collective-permute-done.15 = bf16[16,48,128]{2,1,0:T(8,128)(2,1)S(1)} collective-permute-done((bf16[16,48,128]{2,1,0:T(8,128)(2,1)S(1)}, bf16[16,48,128]{2,1,0:T(8,128)(2,1)S(1)}, u32[]{:S(2)}, u32[]{:S(2)}) %collective-permute-start.15) | collective-permute-done | bytes 196640 | tf_op jit(solution)/shard_map/ppermute | solution.py:68
  70.3 3.2 collective-permute-start.16
  73.6 4.0 %collective-permute-start.3 = (bf16[8,352,128]{2,1,0:T(8,128)(2,1)S(1)}, bf16[8,352,128]{2,1,0:T(8,128)(2,1)S(1)}, u32[]{:S(2)}, u32[]{:S(2)}) collective-permute-start(bf16[8,352,128]{2,1,0:T(8,128)(2,1)S(1)} %pad_maximum_fusion.8), channel_id=1, source_target_pairs={{0,16},{4,20},{8,24},{12,28},{16,0},{20,4},{24,8},{28,12},{32,48},... | collective-permute-start | bytes 2162696 | tf_op jit(solution)/shard_map/ppermute | solution.py:68
  80.1 2.4 collective-permute-done.16
  84.9 8.1 %collective-permute-done.3 = bf16[8,352,128]{2,1,0:T(8,128)(2,1)S(1)} collective-permute-done((bf16[8,352,128]{2,1,0:T(8,128)(2,1)S(1)}, bf16[8,352,128]{2,1,0:T(8,128)(2,1)S(1)}, u32[]{:S(2)}, u32[]{:S(2)}) %collective-permute-start.3) | collective-permute-done | bytes 720928 | tf_op jit(solution)/shard_map/ppermute | solution.py:68
  93.1 5.3 %collective-permute-start.4 = (bf16[16,96,128]{2,1,0:T(8,128)(2,1)S(1)}, bf16[16,96,128]{2,1,0:T(8,128)(2,1)S(1)}, u32[]{:S(2)}, u32[]{:S(2)}) collective-permute-start(bf16[16,96,128]{2,1,0:T(8,128)(2,1)S(1)} %pad_maximum_fusion.20), channel_id=1, source_target_pairs={{0,128},{4,132},{8,136},{12,140},{16,144},{20,148},{24,152},{28,15... | collective-permute-start | bytes 1179656 | tf_op jit(solution)/shard_map/ppermute | solution.py:68
  99.3 2.8 collective-permute-done.19
  103.9 14.1 %collective-permute-done.4 = bf16[16,96,128]{2,1,0:T(8,128)(2,1)S(1)} collective-permute-done((bf16[16,96,128]{2,1,0:T(8,128)(2,1)S(1)}, bf16[16,96,128]{2,1,0:T(8,128)(2,1)S(1)}, u32[]{:S(2)}, u32[]{:S(2)}) %collective-permute-start.4) | collective-permute-done | bytes 393248 | tf_op jit(solution)/shard_map/ppermute | solution.py:68
  119.0 2.2 collective-permute-start.5
  126.5 2.1 copy.224
  128.6 12.0 %collective-permute-done.5 = bf16[32,96,128]{2,1,0:T(8,128)(2,1)} collective-permute-done((bf16[32,96,128]{2,1,0:T(8,128)(2,1)}, bf16[32,96,128]{2,1,0:T(8,128)(2,1)}, u32[]{:S(2)}, u32[]{:S(2)}) %collective-permute-start.5) | collective-permute-done | bytes 786464 | tf_op jit(solution)/shard_map/ppermute | solution.py:68
  140.6 1.8 pad_maximum_fusion.17
  142.5 6.3 %collective-permute-start.6 = (bf16[64,32,128]{2,1,0:T(8,128)(2,1)}, bf16[64,32,128]{2,1,0:T(8,128)(2,1)}, u32[]{:S(2)}, u32[]{:S(2)}) collective-permute-start(bf16[64,32,128]{2,1,0:T(8,128)(2,1)} %pad_maximum_fusion.17), channel_id=1, source_target_pairs={{0,256},{4,260},{8,264},{12,268},{16,272},{20,276},{24,280},{28,28... | collective-permute-start | bytes 1572872 | tf_op jit(solution)/shard_map/ppermute | solution.py:68
  154.4 2.2 copy.226
  156.5 13.8 %collective-permute-done.6 = bf16[64,32,128]{2,1,0:T(8,128)(2,1)} collective-permute-done((bf16[64,32,128]{2,1,0:T(8,128)(2,1)}, bf16[64,32,128]{2,1,0:T(8,128)(2,1)}, u32[]{:S(2)}, u32[]{:S(2)}) %collective-permute-start.6) | collective-permute-done | bytes 524320 | tf_op jit(solution)/shard_map/ppermute | solution.py:68
  181.5 1.8 copy.229
  185.3 1.8 copy.227
  189.2 1.8 copy.225
  191.1 2.3 fusion.146
  193.4 13.3 %psum.7 = f32[4,256]{1,0:T(4,128)S(1)} all-reduce(f32[4,256]{1,0:T(4,128)S(1)} %pad_maximum_fusion.34), channel_id=1, replica_groups=mesh['seq'=128,'head'=4] {'head'}, use_global_device_ids=true, to_apply=%region_24.25 | all-reduce | flops 1024 | bytes 8192 | tf_op jit(solution)/shard_map/psum | solution.py:182
  208.6 1.6 select_reduce_fusion
  215.4 2.3 fusion.43
  222.5 2.4 collective-permute-start.9
  224.9 1.6 fusion.57
  226.6 3.5 collective-permute-done.9
  231.5 1.9 collective-permute-start.10
  233.4 1.9 fusion.63
  236.1 1.8 copy.241
  238.6 1.8 copy.239
  241.2 1.8 copy.237
  243.0 2.1 fusion.31
  247.6 4.1 %collective-permute-start.13 = (bf16[4,224,128]{2,1,0:T(8,128)(2,1)S(1)}, bf16[4,224,128]{2,1,0:T(8,128)(2,1)S(1)}, u32[]{:S(2)}, u32[]{:S(2)}) collective-permute-start(bf16[4,224,128]{2,1,0:T(8,128)(2,1)S(1)} %pad_maximum_fusion.29), channel_id=1, source_target_pairs={{0,32},{4,36},{8,40},{12,44},{16,48},{20,52},{24,56},{28,60},{32,0... | collective-permute-start | bytes 688136 | tf_op jit(solution)/shard_map/ppermute | solution.py:68
  253.4 12.9 %collective-permute-done.13 = bf16[4,224,128]{2,1,0:T(8,128)(2,1)S(1)} collective-permute-done((bf16[4,224,128]{2,1,0:T(8,128)(2,1)S(1)}, bf16[4,224,128]{2,1,0:T(8,128)(2,1)S(1)}, u32[]{:S(2)}, u32[]{:S(2)}) %collective-permute-start.13) | collective-permute-done | bytes 229408 | tf_op jit(solution)/shard_map/ppermute | solution.py:68
  266.4 4.0 %collective-permute-start.14 = (bf16[8,224,128]{2,1,0:T(8,128)(2,1)S(1)}, bf16[8,224,128]{2,1,0:T(8,128)(2,1)S(1)}, u32[]{:S(2)}, u32[]{:S(2)}) collective-permute-start(bf16[8,224,128]{2,1,0:T(8,128)(2,1)S(1)} %pad_maximum_fusion.19), channel_id=1, source_target_pairs={{0,16},{4,20},{8,24},{12,28},{16,0},{20,4},{24,8},{28,12},{32,48},... | collective-permute-start | bytes 1376264 | tf_op jit(solution)/shard_map/ppermute | solution.py:68
  271.0 1.9 subtract_exponential_fusion
  272.9 9.3 %collective-permute-done.14 = bf16[8,224,128]{2,1,0:T(8,128)(2,1)S(1)} collective-permute-done((bf16[8,224,128]{2,1,0:T(8,128)(2,1)S(1)}, bf16[8,224,128]{2,1,0:T(8,128)(2,1)S(1)}, u32[]{:S(2)}, u32[]{:S(2)}) %collective-permute-start.14) | collective-permute-done | bytes 458784 | tf_op jit(solution)/shard_map/ppermute | solution.py:68
  282.2 1.9 collective-permute-start.17
  287.6 10.1 %collective-permute-done.17 = bf16[16,80,128]{2,1,0:T(8,128)(2,1)} collective-permute-done((bf16[16,80,128]{2,1,0:T(8,128)(2,1)S(1)}, bf16[16,80,128]{2,1,0:T(8,128)(2,1)}, u32[]{:S(2)}, u32[]{:S(2)}) %collective-permute-start.17) | collective-permute-done | bytes 327712 | tf_op jit(solution)/shard_map/ppermute | solution.py:68
  297.7 1.9 pad_maximum_fusion.12
  299.6 4.1 %collective-permute-start.18 = (bf16[32,80,128]{2,1,0:T(8,128)(2,1)}, bf16[32,80,128]{2,1,0:T(8,128)(2,1)}, u32[]{:S(2)}, u32[]{:S(2)}) collective-permute-start(bf16[32,80,128]{2,1,0:T(8,128)(2,1)} %pad_maximum_fusion.12), channel_id=1, source_target_pairs={{0,64},{4,68},{8,72},{12,76},{16,80},{20,84},{24,88},{28,92},{32,9... | collective-permute-start | bytes 1966088 | tf_op jit(solution)/shard_map/ppermute | solution.py:68
  303.7 2.2 fusion.6
  305.9 2.3 fusion.45
  308.1 1.6 broadcast_in_dim.676
  309.7 1.8 copy.259
  313.7 4.1 %collective-permute-done.18 = bf16[32,80,128]{2,1,0:T(8,128)(2,1)} collective-permute-done((bf16[32,80,128]{2,1,0:T(8,128)(2,1)}, bf16[32,80,128]{2,1,0:T(8,128)(2,1)}, u32[]{:S(2)}, u32[]{:S(2)}) %collective-permute-start.18) | collective-permute-done | bytes 655392 | tf_op jit(solution)/shard_map/ppermute | solution.py:68
  317.8 2.0 pad_maximum_fusion.16
  321.2 1.6 pad_maximum_fusion.28
  322.8 2.0 copy.293
  332.1 17.7 %collective-permute-done.20 = bf16[64,32,128]{2,1,0:T(8,128)(2,1)} collective-permute-done((bf16[64,32,128]{2,1,0:T(8,128)(2,1)}, bf16[64,32,128]{2,1,0:T(8,128)(2,1)}, u32[]{:S(2)}, u32[]{:S(2)}) %collective-permute-start.20) | collective-permute-done | bytes 524320 | tf_op jit(solution)/shard_map/ppermute | solution.py:68
  349.8 2.2 pad_maximum_fusion.13
  355.8 1.8 convolution_bitcast_fusion.6
  357.7 2.2 fusion.61
  361.4 2.6 fusion.30
  364.0 1.7 copy.282
  (428 shorter events, 101.7 us)
Async XLA Ops:
  0.6 13.5 %copy-start.89 = (s32[4]{0:T(128)S(1)}, s32[4]{0:T(128)}, u32[]{:S(2)}) copy-start(s32[4]{0:T(128)} %constant.134.clone) | copy-start | bytes 52
  0.6 15.5 %copy-start.88 = (s32[16]{0:T(128)S(1)}, s32[16]{0:T(128)}, u32[]{:S(2)}) copy-start(s32[16]{0:T(128)} %constant.135.clone) | copy-start | bytes 196
  1.5 35.7 %copy-start.76 = (pred[32,2]{0,1:T(4,128)(4,1)}, pred[32,2]{0,1:T(4,128)(4,1)S(1)}, u32[]{:S(2)}) copy-start(pred[32,2]{0,1:T(4,128)(4,1)S(1)} %iota_compare_fusion.2) | copy-start | bytes 196
  1.5 16.2 %copy-start.87 = (s32[128]{0:T(128)S(1)}, s32[128]{0:T(128)}, u32[]{:S(2)}) copy-start(s32[128]{0:T(128)} %constant.137.clone) | copy-start | bytes 1540
  2.4 15.4 %copy-start.86 = (s32[64]{0:T(128)S(1)}, s32[64]{0:T(128)}, u32[]{:S(2)}) copy-start(s32[64]{0:T(128)} %constant.136.clone) | copy-start | bytes 772
  5.6 21.0 %copy-start.54 = (bf16[8,2,128]{2,0,1:T(8,128)(2,1)}, bf16[8,2,128]{2,0,1:T(8,128)(2,1)S(1)}, u32[]{:S(2)}) copy-start(bf16[8,2,128]{2,0,1:T(8,128)(2,1)S(1)} %get-tuple-element.25) | copy-start | bytes 12292
  5.7 33.0 %copy-start.74 = (pred[16,2]{0,1:T(4,128)(4,1)}, pred[16,2]{0,1:T(4,128)(4,1)S(1)}, u32[]{:S(2)}) copy-start(pred[16,2]{0,1:T(4,128)(4,1)S(1)} %iota_compare_fusion.1) | copy-start | bytes 100
  7.0 19.6 %copy-start.62 = (bf16[16,2,128]{2,0,1:T(8,128)(2,1)}, bf16[16,2,128]{2,0,1:T(8,128)(2,1)S(1)}, u32[]{:S(2)}) copy-start(bf16[16,2,128]{2,0,1:T(8,128)(2,1)S(1)} %get-tuple-element.24) | copy-start | bytes 24580
  7.1 33.1 %copy-start.72 = (pred[4,2]{0,1:T(4,128)(4,1)}, pred[4,2]{0,1:T(4,128)(4,1)S(1)}, u32[]{:S(2)}) copy-start(pred[4,2]{0,1:T(4,128)(4,1)S(1)} %iota_compare_fusion) | copy-start | bytes 28
  7.7 17.9 %copy-start.31 = (bf16[64,2,128]{2,0,1:T(8,128)(2,1)}, bf16[64,2,128]{2,0,1:T(8,128)(2,1)S(1)}, u32[]{:S(2)}) copy-start(bf16[64,2,128]{2,0,1:T(8,128)(2,1)S(1)} %get-tuple-element.20) | copy-start | bytes 98308
  7.7 17.9 %copy-start.33 = (bf16[64,2,128]{2,0,1:T(8,128)(2,1)}, bf16[64,2,128]{2,0,1:T(8,128)(2,1)S(1)}, u32[]{:S(2)}) copy-start(bf16[64,2,128]{2,0,1:T(8,128)(2,1)S(1)} %get-tuple-element.19) | copy-start | bytes 98308
  7.8 17.9 %copy-start.38 = (bf16[64,2,128]{2,0,1:T(8,128)(2,1)}, bf16[64,2,128]{2,0,1:T(8,128)(2,1)S(1)}, u32[]{:S(2)}) copy-start(bf16[64,2,128]{2,0,1:T(8,128)(2,1)S(1)} %get-tuple-element.21) | copy-start | bytes 98308
  8.0 17.6 %collective-permute-start = (bf16[1,1376,128]{2,1,0:T(8,128)(2,1)S(1)}, bf16[1,1376,128]{2,1,0:T(8,128)(2,1)S(1)}, u32[]{:S(2)}, u32[]{:S(2)}) collective-permute-start(bf16[1,1376,128]{2,1,0:T(8,128)(2,1)S(1)} %bitcast.328), channel_id=1, source_target_pairs={{0,8},{4,12},{8,0},{12,4},{16,24},{20,28},{24,16},{28,20},{32,40},... | collective-permute-start | bytes 1056776 | tf_op jit(solution)/shard_map/ppermute | solution.py:68
  10.6 28.9 %copy-start.40 = (bf16[256,2,128]{2,1,0:T(2,128)(2,1)S(1)}, bf16[256,2,128]{2,1,0:T(2,128)(2,1)}, u32[]{:S(2)}) copy-start(bf16[256,2,128]{2,1,0:T(2,128)(2,1)} %param.13) | copy-start | bytes 393220
  10.6 13.1 %collective-permute-start.7 = (bf16[1,688,128]{2,1,0:T(8,128)(2,1)S(1)}, bf16[1,688,128]{2,1,0:T(8,128)(2,1)S(1)}, u32[]{:S(2)}, u32[]{:S(2)}) collective-permute-start(bf16[1,688,128]{2,1,0:T(8,128)(2,1)S(1)} %maximum_bitcast_fusion), channel_id=1, source_target_pairs={{0,8},{4,12},{8,0},{12,4},{16,24},{20,28},{24,16},{28,20},{32,40},... | collective-permute-start | bytes 528392 | tf_op jit(solution)/shard_map/ppermute | solution.py:68
  23.7 6.0 %collective-permute-start.8 = (bf16[2,688,128]{2,1,0:T(8,128)(2,1)S(1)}, bf16[2,688,128]{2,1,0:T(8,128)(2,1)S(1)}, u32[]{:S(2)}, u32[]{:S(2)}) collective-permute-start(bf16[2,688,128]{2,1,0:T(8,128)(2,1)S(1)} %pad_maximum_fusion.25), channel_id=1, source_target_pairs={{0,4},{4,0},{8,12},{12,8},{16,20},{20,16},{24,28},{28,24},{32,36},... | collective-permute-start | bytes 1056776 | tf_op jit(solution)/shard_map/ppermute | solution.py:68
  26.6 22.2 %collective-permute-start.1 = (bf16[2,1376,128]{2,1,0:T(8,128)(2,1)}, bf16[2,1376,128]{2,1,0:T(8,128)(2,1)S(1)}, u32[]{:S(2)}, u32[]{:S(2)}) collective-permute-start(bf16[2,1376,128]{2,1,0:T(8,128)(2,1)} %pad_maximum_fusion.10), channel_id=1, source_target_pairs={{0,4},{4,0},{8,12},{12,8},{16,20},{20,16},{24,28},{28,24},{32,36},... | collective-permute-start | bytes 2113544 | tf_op jit(solution)/shard_map/ppermute | solution.py:68
  29.7 15.0 %collective-permute-start.11 = (bf16[4,176,128]{2,1,0:T(8,128)(2,1)S(1)}, bf16[4,176,128]{2,1,0:T(8,128)(2,1)S(1)}, u32[]{:S(2)}, u32[]{:S(2)}) collective-permute-start(bf16[4,176,128]{2,1,0:T(8,128)(2,1)S(1)} %pad_maximum_fusion.31), channel_id=1, source_target_pairs={{0,32},{4,36},{8,40},{12,44},{16,48},{20,52},{24,56},{28,60},{32,0... | collective-permute-start | bytes 540680 | tf_op jit(solution)/shard_map/ppermute | solution.py:68
  38.0 205.0 %copy-start.46 = (pred[256,2]{0,1:T(4,128)(4,1)}, pred[256,2]{0,1:T(4,128)(4,1)S(1)}, u32[]{:S(2)}) copy-start(pred[256,2]{0,1:T(4,128)(4,1)S(1)} %broadcast_in_dim.631) | copy-start | bytes 1540
  38.8 152.3 %copy-start.48 = (pred[256,2]{0,1:T(4,128)(4,1)}, pred[256,2]{0,1:T(4,128)(4,1)S(1)}, u32[]{:S(2)}) copy-start(pred[256,2]{0,1:T(4,128)(4,1)S(1)} %broadcast_in_dim.625) | copy-start | bytes 1540
  44.7 12.8 %collective-permute-start.12 = (bf16[8,176,128]{2,1,0:T(8,128)(2,1)S(1)}, bf16[8,176,128]{2,1,0:T(8,128)(2,1)S(1)}, u32[]{:S(2)}, u32[]{:S(2)}) collective-permute-start(bf16[8,176,128]{2,1,0:T(8,128)(2,1)S(1)} %pad_maximum_fusion.24), channel_id=1, source_target_pairs={{0,16},{4,20},{8,24},{12,28},{16,0},{20,4},{24,8},{28,12},{32,48},... | collective-permute-start | bytes 1081352 | tf_op jit(solution)/shard_map/ppermute | solution.py:68
  49.0 24.5 %collective-permute-start.2 = (bf16[4,352,128]{2,1,0:T(8,128)(2,1)S(1)}, bf16[4,352,128]{2,1,0:T(8,128)(2,1)S(1)}, u32[]{:S(2)}, u32[]{:S(2)}) collective-permute-start(bf16[4,352,128]{2,1,0:T(8,128)(2,1)S(1)} %pad_maximum_fusion.23), channel_id=1, source_target_pairs={{0,32},{4,36},{8,40},{12,44},{16,48},{20,52},{24,56},{28,60},{32,0... | collective-permute-start | bytes 1081352 | tf_op jit(solution)/shard_map/ppermute | solution.py:68
  58.4 24.1 %copy-start.11 = (bf16[16,48,128]{2,1,0:T(8,128)(2,1)}, bf16[16,48,128]{2,1,0:T(8,128)(2,1)S(1)}, u32[]{:S(2)}) copy-start(bf16[16,48,128]{2,1,0:T(8,128)(2,1)S(1)} %pad_maximum_fusion.30) | copy-start | bytes 589828
  58.4 11.9 %collective-permute-start.15 = (bf16[16,48,128]{2,1,0:T(8,128)(2,1)S(1)}, bf16[16,48,128]{2,1,0:T(8,128)(2,1)S(1)}, u32[]{:S(2)}, u32[]{:S(2)}) collective-permute-start(bf16[16,48,128]{2,1,0:T(8,128)(2,1)S(1)} %pad_maximum_fusion.30), channel_id=1, source_target_pairs={{0,128},{4,132},{8,136},{12,140},{16,144},{20,148},{24,152},{28,15... | collective-permute-start | bytes 589832 | tf_op jit(solution)/shard_map/ppermute | solution.py:68
  66.5 11.2 %copy-start.16 = (bf16[4,1,256,2,128]{4,2,0,3,1:T(8,128)(2,1)S(1)}, bf16[4,1,256,2,128]{4,2,0,3,1:T(8,128)(2,1)}, u32[]{:S(2)}) copy-start(bf16[4,1,256,2,128]{4,2,0,3,1:T(8,128)(2,1)} %copy.211) | copy-start | bytes 1572868
  70.3 12.2 %collective-permute-start.16 = (bf16[32,48,128]{2,1,0:T(8,128)(2,1)S(1)}, bf16[32,48,128]{2,1,0:T(8,128)(2,1)S(1)}, u32[]{:S(2)}, u32[]{:S(2)}) collective-permute-start(bf16[32,48,128]{2,1,0:T(8,128)(2,1)S(1)} %pad_maximum_fusion.22), channel_id=1, source_target_pairs={{0,64},{4,68},{8,72},{12,76},{16,80},{20,84},{24,88},{28,92},{32,9... | collective-permute-start | bytes 1179656 | tf_op jit(solution)/shard_map/ppermute | solution.py:68
  73.6 19.4 %collective-permute-start.3 = (bf16[8,352,128]{2,1,0:T(8,128)(2,1)S(1)}, bf16[8,352,128]{2,1,0:T(8,128)(2,1)S(1)}, u32[]{:S(2)}, u32[]{:S(2)}) collective-permute-start(bf16[8,352,128]{2,1,0:T(8,128)(2,1)S(1)} %pad_maximum_fusion.8), channel_id=1, source_target_pairs={{0,16},{4,20},{8,24},{12,28},{16,0},{20,4},{24,8},{28,12},{32,48},... | collective-permute-start | bytes 2162696 | tf_op jit(solution)/shard_map/ppermute | solution.py:68
  80.1 13.0 %copy-start.9 = (bf16[4,352,128]{2,1,0:T(8,128)(2,1)S(1)}, bf16[4,352,128]{2,1,0:T(8,128)(2,1)}, u32[]{:S(2)}) copy-start(bf16[4,352,128]{2,1,0:T(8,128)(2,1)} %copy-done.8) | copy-start | bytes 1081348
  82.5 15.9 %copy-start.12 = (bf16[16,48,128]{2,1,0:T(8,128)(2,1)S(1)}, bf16[16,48,128]{2,1,0:T(8,128)(2,1)}, u32[]{:S(2)}) copy-start(bf16[16,48,128]{2,1,0:T(8,128)(2,1)} %copy-done.11) | copy-start | bytes 589828
  82.5 19.5 %collective-permute-start.19 = (bf16[64,16,128]{2,1,0:T(8,128)(2,1)S(1)}, bf16[64,16,128]{2,1,0:T(8,128)(2,1)S(1)}, u32[]{:S(2)}, u32[]{:S(2)}) collective-permute-start(bf16[64,16,128]{2,1,0:T(8,128)(2,1)S(1)} %pad_maximum_fusion.27), channel_id=1, source_target_pairs={{256,0},{260,4},{264,8},{268,12},{272,16},{276,20},{280,24},{284,2... | collective-permute-start | bytes 786440 | tf_op jit(solution)/shard_map/ppermute | solution.py:68
  93.1 24.9 %collective-permute-start.4 = (bf16[16,96,128]{2,1,0:T(8,128)(2,1)S(1)}, bf16[16,96,128]{2,1,0:T(8,128)(2,1)S(1)}, u32[]{:S(2)}, u32[]{:S(2)}) collective-permute-start(bf16[16,96,128]{2,1,0:T(8,128)(2,1)S(1)} %pad_maximum_fusion.20), channel_id=1, source_target_pairs={{0,128},{4,132},{8,136},{12,140},{16,144},{20,148},{24,152},{28,15... | collective-permute-start | bytes 1179656 | tf_op jit(solution)/shard_map/ppermute | solution.py:68
  103.8 19.2 %copy-start.34 = (bf16[64,2,128]{2,0,1:T(8,128)(2,1)S(1)}, bf16[64,2,128]{2,0,1:T(8,128)(2,1)}, u32[]{:S(2)}) copy-start(bf16[64,2,128]{2,0,1:T(8,128)(2,1)} %copy-done.33) | copy-start | bytes 98308
  103.8 19.2 %copy-start.37 = (pred[64,1024]{1,0:T(8,128)(4,1)S(1)}, pred[64,1024]{1,0:T(8,128)(4,1)}, u32[]{:S(2)}) copy-start(pred[64,1024]{1,0:T(8,128)(4,1)} %broadcast_compare_fusion.3) | copy-start | bytes 196612
  119.0 21.7 %collective-permute-start.5 = (bf16[32,96,128]{2,1,0:T(8,128)(2,1)}, bf16[32,96,128]{2,1,0:T(8,128)(2,1)}, u32[]{:S(2)}, u32[]{:S(2)}) collective-permute-start(bf16[32,96,128]{2,1,0:T(8,128)(2,1)} %pad_maximum_fusion.5), channel_id=1, source_target_pairs={{0,64},{4,68},{8,72},{12,76},{16,80},{20,84},{24,88},{28,92},{32,9... | collective-permute-start | bytes 2359304 | tf_op jit(solution)/shard_map/ppermute | solution.py:68
  126.5 22.3 %copy-start.4 = (bf16[16,96,128]{2,1,0:T(8,128)(2,1)S(1)}, bf16[16,96,128]{2,1,0:T(8,128)(2,1)}, u32[]{:S(2)}) copy-start(bf16[16,96,128]{2,1,0:T(8,128)(2,1)} %copy-done.3) | copy-start | bytes 1179652
  142.5 27.8 %collective-permute-start.6 = (bf16[64,32,128]{2,1,0:T(8,128)(2,1)}, bf16[64,32,128]{2,1,0:T(8,128)(2,1)}, u32[]{:S(2)}, u32[]{:S(2)}) collective-permute-start(bf16[64,32,128]{2,1,0:T(8,128)(2,1)} %pad_maximum_fusion.17), channel_id=1, source_target_pairs={{0,256},{4,260},{8,264},{12,268},{16,272},{20,276},{24,280},{28,28... | collective-permute-start | bytes 1572872 | tf_op jit(solution)/shard_map/ppermute | solution.py:68
  153.5 16.8 %copy-start.70 = (f32[16,2]{0,1:T(2,128)}, f32[16,2]{0,1:T(2,128)S(1)}, u32[]{:S(2)}) copy-start(f32[16,2]{0,1:T(2,128)S(1)} %add_bitcast_fusion.2) | copy-start | bytes 388
  174.7 16.3 %copy-start.56 = (f32[256,2]{0,1:T(2,128)}, f32[256,2]{0,1:T(2,128)S(1)}, u32[]{:S(2)}) copy-start(f32[256,2]{0,1:T(2,128)S(1)} %get-tuple-element.30) | copy-start | bytes 6148
  177.9 11.3 %copy-start.64 = (f32[16,2]{0,1:T(2,128)}, f32[16,2]{0,1:T(2,128)S(1)}, u32[]{:S(2)}) copy-start(f32[16,2]{0,1:T(2,128)S(1)} %get-tuple-element.72) | copy-start | bytes 388
  191.0 17.6 %copy-start.77 = (pred[32,2]{0,1:T(4,128)(4,1)S(1)}, pred[32,2]{0,1:T(4,128)(4,1)}, u32[]{:S(2)}) copy-start(pred[32,2]{0,1:T(4,128)(4,1)} %copy-done.76) | copy-start | bytes 196
  191.1 19.2 %copy-start.75 = (pred[16,2]{0,1:T(4,128)(4,1)S(1)}, pred[16,2]{0,1:T(4,128)(4,1)}, u32[]{:S(2)}) copy-start(pred[16,2]{0,1:T(4,128)(4,1)} %copy-done.74) | copy-start | bytes 100
  191.1 22.5 %copy-start.73 = (pred[4,2]{0,1:T(4,128)(4,1)S(1)}, pred[4,2]{0,1:T(4,128)(4,1)}, u32[]{:S(2)}) copy-start(pred[4,2]{0,1:T(4,128)(4,1)} %copy-done.72) | copy-start | bytes 28
  207.9 10.6 %copy-start.20 = (bf16[256,2,128]{0,2,1:T(8,128)(2,1)}, bf16[256,2,128]{0,2,1:T(8,128)(2,1)S(1)}, u32[]{:S(2)}) copy-start(bf16[256,2,128]{0,2,1:T(8,128)(2,1)S(1)} %get-tuple-element.29) | copy-start | bytes 393220
  222.5 24.2 %copy-start.10 = (bf16[768,128]{1,0:T(8,128)(2,1)}, bf16[768,128]{1,0:T(8,128)(2,1)S(1)}, u32[]{:S(2)}) copy-start(bf16[768,128]{1,0:T(8,128)(2,1)S(1)} %constant_dynamic-update-slice_fusion.8) | copy-start | bytes 589828
  222.5 7.6 %collective-permute-start.9 = (bf16[1,768,128]{2,1,0:T(8,128)(2,1)S(1)}, bf16[1,768,128]{2,1,0:T(8,128)(2,1)S(1)}, u32[]{:S(2)}, u32[]{:S(2)}) collective-permute-start(bf16[1,768,128]{2,1,0:T(8,128)(2,1)S(1)} %bitcast.332), channel_id=1, source_target_pairs={{0,8},{4,12},{8,0},{12,4},{16,24},{20,28},{24,16},{28,20},{32,40},... | collective-permute-start | bytes 589832 | tf_op jit(solution)/shard_map/ppermute | solution.py:68
  226.5 13.9 %copy-start.35 = (f32[64,2,128]{2,0,1:T(8,128)S(1)}, f32[64,2,128]{2,0,1:T(8,128)}, u32[]{:S(2)}) copy-start(f32[64,2,128]{2,0,1:T(8,128)} %fusion.43) | copy-start | bytes 196612
  226.5 16.4 %copy-start.21 = (bf16[256,2,128]{0,2,1:T(8,128)(2,1)S(1)}, bf16[256,2,128]{0,2,1:T(8,128)(2,1)}, u32[]{:S(2)}) copy-start(bf16[256,2,128]{0,2,1:T(8,128)(2,1)} %copy-done.20) | copy-start | bytes 393220
  226.5 16.4 %copy-start.49 = (pred[256,2]{0,1:T(4,128)(4,1)S(1)}, pred[256,2]{0,1:T(4,128)(4,1)}, u32[]{:S(2)}) copy-start(pred[256,2]{0,1:T(4,128)(4,1)} %copy-done.48) | copy-start | bytes 1540
  226.5 16.4 %copy-start.52 = (pred[256,2]{0,1:T(4,128)(4,1)S(1)}, pred[256,2]{0,1:T(4,128)(4,1)}, u32[]{:S(2)}) copy-start(pred[256,2]{0,1:T(4,128)(4,1)} %broadcast_in_dim.618) | copy-start | bytes 1540
  226.6 16.4 %copy-start.57 = (f32[256,2]{0,1:T(2,128)S(1)}, f32[256,2]{0,1:T(2,128)}, u32[]{:S(2)}) copy-start(f32[256,2]{0,1:T(2,128)} %copy-done.56) | copy-start | bytes 6148
  231.5 14.4 %collective-permute-start.10 = (bf16[2,768,128]{2,1,0:T(8,128)(2,1)}, bf16[2,768,128]{2,1,0:T(8,128)(2,1)S(1)}, u32[]{:S(2)}, u32[]{:S(2)}) collective-permute-start(bf16[2,768,128]{2,1,0:T(8,128)(2,1)} %pad_maximum_fusion.21), channel_id=1, source_target_pairs={{0,4},{4,0},{8,12},{12,8},{16,20},{20,16},{24,28},{28,24},{32,36},... | collective-permute-start | bytes 1179656 | tf_op jit(solution)/shard_map/ppermute | solution.py:68
  247.6 18.7 %collective-permute-start.13 = (bf16[4,224,128]{2,1,0:T(8,128)(2,1)S(1)}, bf16[4,224,128]{2,1,0:T(8,128)(2,1)S(1)}, u32[]{:S(2)}, u32[]{:S(2)}) collective-permute-start(bf16[4,224,128]{2,1,0:T(8,128)(2,1)S(1)} %pad_maximum_fusion.29), channel_id=1, source_target_pairs={{0,32},{4,36},{8,40},{12,44},{16,48},{20,52},{24,56},{28,60},{32,0... | collective-permute-start | bytes 688136 | tf_op jit(solution)/shard_map/ppermute | solution.py:68
  251.7 19.3 %copy-start.19 = (bf16[256,2,128]{2,1,0:T(2,128)(2,1)S(1)}, bf16[256,2,128]{2,1,0:T(2,128)(2,1)}, u32[]{:S(2)}) copy-start(bf16[256,2,128]{2,1,0:T(2,128)(2,1)} %param.11) | copy-start | bytes 393220
  266.4 15.8 %collective-permute-start.14 = (bf16[8,224,128]{2,1,0:T(8,128)(2,1)S(1)}, bf16[8,224,128]{2,1,0:T(8,128)(2,1)S(1)}, u32[]{:S(2)}, u32[]{:S(2)}) collective-permute-start(bf16[8,224,128]{2,1,0:T(8,128)(2,1)S(1)} %pad_maximum_fusion.19), channel_id=1, source_target_pairs={{0,16},{4,20},{8,24},{12,28},{16,0},{20,4},{24,8},{28,12},{32,48},... | collective-permute-start | bytes 1376264 | tf_op jit(solution)/shard_map/ppermute | solution.py:68
  282.2 15.5 %collective-permute-start.17 = (bf16[16,80,128]{2,1,0:T(8,128)(2,1)S(1)}, bf16[16,80,128]{2,1,0:T(8,128)(2,1)}, u32[]{:S(2)}, u32[]{:S(2)}) collective-permute-start(bf16[16,80,128]{2,1,0:T(8,128)(2,1)S(1)} %pad_maximum_fusion.26), channel_id=1, source_target_pairs={{0,128},{4,132},{8,136},{12,140},{16,144},{20,148},{24,152},{28,15... | collective-permute-start | bytes 983048 | tf_op jit(solution)/shard_map/ppermute | solution.py:68
  285.7 18.0 %copy-start.39 = (bf16[64,2,128]{2,0,1:T(8,128)(2,1)S(1)}, bf16[64,2,128]{2,0,1:T(8,128)(2,1)}, u32[]{:S(2)}) copy-start(bf16[64,2,128]{2,0,1:T(8,128)(2,1)} %copy-done.38) | copy-start | bytes 98308
  286.8 19.0 %copy-start.32 = (bf16[64,2,128]{2,0,1:T(8,128)(2,1)S(1)}, bf16[64,2,128]{2,0,1:T(8,128)(2,1)}, u32[]{:S(2)}) copy-start(bf16[64,2,128]{2,0,1:T(8,128)(2,1)} %copy-done.31) | copy-start | bytes 98308
  287.6 18.3 %copy-start.58 = (f32[2,1024]{1,0:T(2,128)S(1)}, f32[2,1024]{1,0:T(2,128)}, u32[]{:S(2)}) copy-start(f32[2,1024]{1,0:T(2,128)} %sub.438) | copy-start | bytes 24580
  299.6 18.2 %collective-permute-start.18 = (bf16[32,80,128]{2,1,0:T(8,128)(2,1)}, bf16[32,80,128]{2,1,0:T(8,128)(2,1)}, u32[]{:S(2)}, u32[]{:S(2)}) collective-permute-start(bf16[32,80,128]{2,1,0:T(8,128)(2,1)} %pad_maximum_fusion.12), channel_id=1, source_target_pairs={{0,64},{4,68},{8,72},{12,76},{16,80},{20,84},{24,88},{28,92},{32,9... | collective-permute-start | bytes 1966088 | tf_op jit(solution)/shard_map/ppermute | solution.py:68
  313.7 12.2 %copy-start.63 = (bf16[16,2,128]{2,0,1:T(8,128)(2,1)S(1)}, bf16[16,2,128]{2,0,1:T(8,128)(2,1)}, u32[]{:S(2)}) copy-start(bf16[16,2,128]{2,0,1:T(8,128)(2,1)} %copy-done.62) | copy-start | bytes 24580
  313.7 12.2 %copy-start.71 = (pred[1024,16]{0,1:T(8,128)(4,1)S(1)}, pred[1024,16]{0,1:T(8,128)(4,1)}, u32[]{:S(2)}) copy-start(pred[1024,16]{0,1:T(8,128)(4,1)} %broadcast_compare_fusion.4) | copy-start | bytes 49156
  319.8 30.0 %collective-permute-start.20 = (bf16[64,32,128]{2,1,0:T(8,128)(2,1)}, bf16[64,32,128]{2,1,0:T(8,128)(2,1)}, u32[]{:S(2)}, u32[]{:S(2)}) collective-permute-start(bf16[64,32,128]{2,1,0:T(8,128)(2,1)} %get-tuple-element.33), channel_id=1, source_target_pairs={{256,0},{260,4},{264,8},{268,12},{272,16},{276,20},{280,24},{284,2... | collective-permute-start | bytes 1572872 | tf_op jit(solution)/shard_map/ppermute | solution.py:68
  332.1 22.4 %copy-start.69 = (bf16[8,2,128]{2,0,1:T(8,128)(2,1)S(1)}, bf16[8,2,128]{2,0,1:T(8,128)(2,1)}, u32[]{:S(2)}) copy-start(bf16[8,2,128]{2,0,1:T(8,128)(2,1)} %copy-done.68) | copy-start | bytes 12292
  332.1 22.4 %copy-start.80 = (pred[1024,8]{0,1:T(8,128)(4,1)S(1)}, pred[1024,8]{0,1:T(8,128)(4,1)}, u32[]{:S(2)}) copy-start(pred[1024,8]{0,1:T(8,128)(4,1)} %broadcast_compare_fusion.6) | copy-start | bytes 24580
  (47 other events, 212.2 us)
where the time goes:
time: 371 us; the launch traced here: 369 us
  waiting for transfers between devices  123 us (33%)
  starting transfers between devices  76.5 us (21%)
  local copies, waits for them, and re-layouts  70 us (19%)
  other arithmetic  46.2 us (12%)
  matrix products  37.5 us (10%)
  blocking collectives  13.3 us (4%)
    ppermute x21, waiting for transfers between devices, extend(): moved = lax.ppermute(state, 'seq', pairs)  123 us
    ppermute x21, starting transfers between devices, extend(): moved = lax.ppermute(state, 'seq', pairs)  76.5 us
    broadcast_in_dim x45, local copies, waits for them, and re-layouts, put_rows(): jnp.where(column == target, compact[:, None], jnp.asarray(filler, compact...  30.1 us
    psum x1, blocking collectives, shards(): lax.psum(jnp.stack([jnp.sum(attended, axis=(1, 2)), jnp.sum(attended * at...  13.3 us
    concatenate x20, other arithmetic, extend(): state = jnp.concatenate([state, moved], axis=0)  13.2 us
    unnamed x205, local copies, waits for them, and re-layouts  12.9 us
    reduce_sum x12, other arithmetic, pick_rows(): return jnp.sum(zeroed, axis=1, dtype=source.dtype)  12.1 us
    dot_general x4, matrix products, shards(): jnp.einsum('hqk,qhd->khd', score_grad, queries, preferred_element_type=jn...  8.41 us
  transfers between devices with their start and end apart: 21, of which 16 were waited for; matrix products, arithmetic and copies ran while one was open for 21% of the time, Pallas kernels for 0%

commit v1 on v0

--- a/solution.py
+++ b/solution.py
@@ -179,16 +179,19 @@
         )
         attended = attended + put_rows(out_sel, level["wanted"], level["stride"], 0.0)
     grad_in = cotangent.astype(jnp.float32) * norm_gain[None]
-    sums = lax.psum(
-        jnp.stack(
-            [
-                jnp.sum(attended, axis=(1, 2)),
-                jnp.sum(attended * attended, axis=(1, 2)),
-                jnp.sum(grad_in, axis=(1, 2)),
-                jnp.sum(grad_in * attended, axis=(1, 2)),
-            ]
+    sums = jnp.sum(
+        lax.all_gather(
+            jnp.stack(
+                [
+                    jnp.sum(attended, axis=(1, 2)),
+                    jnp.sum(attended * attended, axis=(1, 2)),
+                    jnp.sum(grad_in, axis=(1, 2)),
+                    jnp.sum(grad_in * attended, axis=(1, 2)),
+                ]
+            ),
+            "head",
         ),
-        "head",
+        axis=0,
     )
     centre = sums[0] / features
     variance = sums[1] / features - centre * centre

time: 371 us -> 375 us (1.011)
  the two profiles are of different devices: /device:TPU:74 before, /device:TPU:68 now
where the time goes in v1:
time: 375 us; the launch traced here: 372 us
  waiting for transfers between devices  113 us (30%)
  starting transfers between devices  79 us (21%)
  local copies, waits for them, and re-layouts  69.4 us (19%)
  other arithmetic  46.2 us (12%)
  matrix products  37.5 us (10%)
  blocking collectives  24.8 us (7%)
    ppermute x21, waiting for transfers between devices, extend(): moved = lax.ppermute(state, 'seq', pairs)  113 us
    ppermute x21, starting transfers between devices, extend(): moved = lax.ppermute(state, 'seq', pairs)  79 us
    broadcast_in_dim x45, local copies, waits for them, and re-layouts, put_rows(): jnp.where(column == target, compact[:, None], jnp.asarray(filler, compact...  30.1 us
    all_gather x1, blocking collectives, shards(): lax.all_gather(jnp.stack([jnp.sum(attended, axis=(1, 2)), jnp.sum(attende...  24.8 us
    concatenate x20, other arithmetic, extend(): state = jnp.concatenate([state, moved], axis=0)  13.2 us
    unnamed x205, local copies, waits for them, and re-layouts  12.3 us
    reduce_sum x12, other arithmetic, pick_rows(): return jnp.sum(zeroed, axis=1, dtype=source.dtype)  12.1 us
    dot_general x4, matrix products, shards(): jnp.einsum('hqk,qhd->khd', score_grad, queries, preferred_element_type=jn...  8.4 us
  transfers between devices with their start and end apart: 21, of which 15 were waited for; matrix products, arithmetic and copies ran while one was open for 21% of the time, Pallas kernels for 0%

profile of v1, /device:TPU:68, one launch (start us, length us, event | category | flops | bytes accessed | tf_op | source)
XLA Modules:
  0.0 372.2 jit_solution(11523083052807177934)
XLA Ops:
  8.0 3.1 collective-permute-start
  11.2 2.9 collective-permute-start.7
  19.5 4.2 %collective-permute-done.7 = bf16[1,688,128]{2,1,0:T(8,128)(2,1)S(1)} collective-permute-done((bf16[1,688,128]{2,1,0:T(8,128)(2,1)S(1)}, bf16[1,688,128]{2,1,0:T(8,128)(2,1)S(1)}, u32[]{:S(2)}, u32[]{:S(2)}) %collective-permute-start.7) | collective-permute-done | bytes 176160 | tf_op jit(solution)/shard_map/ppermute | solution.py:68
  23.7 1.9 collective-permute-start.8
  26.6 2.4 collective-permute-start.1
  29.7 7.7 %collective-permute-start.11 = (bf16[4,176,128]{2,1,0:T(8,128)(2,1)S(1)}, bf16[4,176,128]{2,1,0:T(8,128)(2,1)S(1)}, u32[]{:S(2)}, u32[]{:S(2)}) collective-permute-start(bf16[4,176,128]{2,1,0:T(8,128)(2,1)S(1)} %pad_maximum_fusion.31), channel_id=1, source_target_pairs={{0,32},{4,36},{8,40},{12,44},{16,48},{20,52},{24,56},{28,60},{32,0... | collective-permute-start | bytes 540680 | tf_op jit(solution)/shard_map/ppermute | solution.py:68
  43.1 2.1 collective-permute-done.11
  45.3 2.4 collective-permute-start.12
  48.0 8.3 %collective-permute-start.2 = (bf16[4,352,128]{2,1,0:T(8,128)(2,1)S(1)}, bf16[4,352,128]{2,1,0:T(8,128)(2,1)S(1)}, u32[]{:S(2)}, u32[]{:S(2)}) collective-permute-start(bf16[4,352,128]{2,1,0:T(8,128)(2,1)S(1)} %pad_maximum_fusion.23), channel_id=1, source_target_pairs={{0,32},{4,36},{8,40},{12,44},{16,48},{20,52},{24,56},{28,60},{32,0... | collective-permute-start | bytes 1081352 | tf_op jit(solution)/shard_map/ppermute | solution.py:68
  57.4 6.1 %collective-permute-start.15 = (bf16[16,48,128]{2,1,0:T(8,128)(2,1)S(1)}, bf16[16,48,128]{2,1,0:T(8,128)(2,1)S(1)}, u32[]{:S(2)}, u32[]{:S(2)}) collective-permute-start(bf16[16,48,128]{2,1,0:T(8,128)(2,1)S(1)} %pad_maximum_fusion.30), channel_id=1, source_target_pairs={{0,128},{4,132},{8,136},{12,140},{16,144},{20,148},{24,152},{28,15... | collective-permute-start | bytes 589832 | tf_op jit(solution)/shard_map/ppermute | solution.py:68
  65.6 2.3 collective-permute-done.15
  67.9 3.6 collective-permute-start.16
  71.7 4.0 %collective-permute-start.3 = (bf16[8,352,128]{2,1,0:T(8,128)(2,1)S(1)}, bf16[8,352,128]{2,1,0:T(8,128)(2,1)S(1)}, u32[]{:S(2)}, u32[]{:S(2)}) collective-permute-start(bf16[8,352,128]{2,1,0:T(8,128)(2,1)S(1)} %pad_maximum_fusion.8), channel_id=1, source_target_pairs={{0,16},{4,20},{8,24},{12,28},{16,0},{20,4},{24,8},{28,12},{32,48},... | collective-permute-start | bytes 2162696 | tf_op jit(solution)/shard_map/ppermute | solution.py:68
  80.5 8.8 %collective-permute-done.3 = bf16[8,352,128]{2,1,0:T(8,128)(2,1)S(1)} collective-permute-done((bf16[8,352,128]{2,1,0:T(8,128)(2,1)S(1)}, bf16[8,352,128]{2,1,0:T(8,128)(2,1)S(1)}, u32[]{:S(2)}, u32[]{:S(2)}) %collective-permute-start.3) | collective-permute-done | bytes 720928 | tf_op jit(solution)/shard_map/ppermute | solution.py:68
  89.4 3.2 collective-permute-start.4
  93.5 1.9 collective-permute-done.19
  97.2 11.2 %collective-permute-done.4 = bf16[16,96,128]{2,1,0:T(8,128)(2,1)S(1)} collective-permute-done((bf16[16,96,128]{2,1,0:T(8,128)(2,1)S(1)}, bf16[16,96,128]{2,1,0:T(8,128)(2,1)S(1)}, u32[]{:S(2)}, u32[]{:S(2)}) %collective-permute-start.4) | collective-permute-done | bytes 393248 | tf_op jit(solution)/shard_map/ppermute | solution.py:68
  109.4 4.2 %collective-permute-start.5 = (bf16[32,96,128]{2,1,0:T(8,128)(2,1)}, bf16[32,96,128]{2,1,0:T(8,128)(2,1)}, u32[]{:S(2)}, u32[]{:S(2)}) collective-permute-start(bf16[32,96,128]{2,1,0:T(8,128)(2,1)} %pad_maximum_fusion.5), channel_id=1, source_target_pairs={{0,64},{4,68},{8,72},{12,76},{16,80},{20,84},{24,88},{28,92},{32,9... | collective-permute-start | bytes 2359304 | tf_op jit(solution)/shard_map/ppermute | solution.py:68
  118.9 2.1 copy.224
  121.1 10.1 %collective-permute-done.5 = bf16[32,96,128]{2,1,0:T(8,128)(2,1)} collective-permute-done((bf16[32,96,128]{2,1,0:T(8,128)(2,1)}, bf16[32,96,128]{2,1,0:T(8,128)(2,1)}, u32[]{:S(2)}, u32[]{:S(2)}) %collective-permute-start.5) | collective-permute-done | bytes 786464 | tf_op jit(solution)/shard_map/ppermute | solution.py:68
  131.2 1.8 pad_maximum_fusion.17
  133.0 8.8 %collective-permute-start.6 = (bf16[64,32,128]{2,1,0:T(8,128)(2,1)}, bf16[64,32,128]{2,1,0:T(8,128)(2,1)}, u32[]{:S(2)}, u32[]{:S(2)}) collective-permute-start(bf16[64,32,128]{2,1,0:T(8,128)(2,1)} %pad_maximum_fusion.17), channel_id=1, source_target_pairs={{0,256},{4,260},{8,264},{12,268},{16,272},{20,276},{24,280},{28,28... | collective-permute-start | bytes 1572872 | tf_op jit(solution)/shard_map/ppermute | solution.py:68
  147.4 2.2 copy.226
  149.6 13.5 %collective-permute-done.6 = bf16[64,32,128]{2,1,0:T(8,128)(2,1)} collective-permute-done((bf16[64,32,128]{2,1,0:T(8,128)(2,1)}, bf16[64,32,128]{2,1,0:T(8,128)(2,1)}, u32[]{:S(2)}, u32[]{:S(2)}) %collective-permute-start.6) | collective-permute-done | bytes 524320 | tf_op jit(solution)/shard_map/ppermute | solution.py:68
  168.0 1.5 fusion.111
  173.7 1.8 copy.229
  177.5 1.8 copy.227
  181.4 1.8 copy.225
  183.3 2.4 fusion.146
  185.7 24.8 %all-gather.1 = f32[4,4,256]{2,1,0:T(4,128)S(1)} all-gather(f32[1,4,256]{2,1,0:T(4,128)S(1)} %maximum_bitcast_fusion.2), channel_id=2, replica_groups=mesh['seq'=128,'head'=4] {'head'}, dimensions={0}, use_global_device_ids=true | all-gather | bytes 20480 | tf_op jit(solution)/shard_map/all_gather | solution.py:183
  212.4 1.6 select_reduce_fusion
  219.2 2.3 fusion.43
  226.3 3.1 collective-permute-start.9
  229.4 1.6 fusion.57
  231.0 2.8 collective-permute-done.9
  235.3 1.9 collective-permute-start.10
  237.2 1.9 fusion.63
  239.9 1.8 copy.241
  242.4 1.8 copy.239
  244.9 1.8 copy.237
  246.7 2.1 fusion.31
  251.4 4.1 %collective-permute-start.13 = (bf16[4,224,128]{2,1,0:T(8,128)(2,1)S(1)}, bf16[4,224,128]{2,1,0:T(8,128)(2,1)S(1)}, u32[]{:S(2)}, u32[]{:S(2)}) collective-permute-start(bf16[4,224,128]{2,1,0:T(8,128)(2,1)S(1)} %pad_maximum_fusion.29), channel_id=1, source_target_pairs={{0,32},{4,36},{8,40},{12,44},{16,48},{20,52},{24,56},{28,60},{32,0... | collective-permute-start | bytes 688136 | tf_op jit(solution)/shard_map/ppermute | solution.py:68
  257.2 12.8 %collective-permute-done.13 = bf16[4,224,128]{2,1,0:T(8,128)(2,1)S(1)} collective-permute-done((bf16[4,224,128]{2,1,0:T(8,128)(2,1)S(1)}, bf16[4,224,128]{2,1,0:T(8,128)(2,1)S(1)}, u32[]{:S(2)}, u32[]{:S(2)}) %collective-permute-start.13) | collective-permute-done | bytes 229408 | tf_op jit(solution)/shard_map/ppermute | solution.py:68
  270.0 2.4 collective-permute-start.14
  273.1 1.9 subtract_exponential_fusion
  274.9 10.9 %collective-permute-done.14 = bf16[8,224,128]{2,1,0:T(8,128)(2,1)S(1)} collective-permute-done((bf16[8,224,128]{2,1,0:T(8,128)(2,1)S(1)}, bf16[8,224,128]{2,1,0:T(8,128)(2,1)S(1)}, u32[]{:S(2)}, u32[]{:S(2)}) %collective-permute-start.14) | collective-permute-done | bytes 458784 | tf_op jit(solution)/shard_map/ppermute | solution.py:68
  285.9 1.9 collective-permute-start.17
  291.3 10.1 %collective-permute-done.17 = bf16[16,80,128]{2,1,0:T(8,128)(2,1)} collective-permute-done((bf16[16,80,128]{2,1,0:T(8,128)(2,1)S(1)}, bf16[16,80,128]{2,1,0:T(8,128)(2,1)}, u32[]{:S(2)}, u32[]{:S(2)}) %collective-permute-start.17) | collective-permute-done | bytes 327712 | tf_op jit(solution)/shard_map/ppermute | solution.py:68
  301.4 1.9 pad_maximum_fusion.12
  303.3 4.1 %collective-permute-start.18 = (bf16[32,80,128]{2,1,0:T(8,128)(2,1)}, bf16[32,80,128]{2,1,0:T(8,128)(2,1)}, u32[]{:S(2)}, u32[]{:S(2)}) collective-permute-start(bf16[32,80,128]{2,1,0:T(8,128)(2,1)} %pad_maximum_fusion.12), channel_id=1, source_target_pairs={{0,64},{4,68},{8,72},{12,76},{16,80},{20,84},{24,88},{28,92},{32,9... | collective-permute-start | bytes 1966088 | tf_op jit(solution)/shard_map/ppermute | solution.py:68
  307.4 2.2 fusion.6
  309.6 2.3 fusion.45
  311.9 1.6 broadcast_in_dim.676
  313.5 1.8 copy.259
  317.5 4.1 %collective-permute-done.18 = bf16[32,80,128]{2,1,0:T(8,128)(2,1)} collective-permute-done((bf16[32,80,128]{2,1,0:T(8,128)(2,1)}, bf16[32,80,128]{2,1,0:T(8,128)(2,1)}, u32[]{:S(2)}, u32[]{:S(2)}) %collective-permute-start.18) | collective-permute-done | bytes 655392 | tf_op jit(solution)/shard_map/ppermute | solution.py:68
  321.5 2.0 pad_maximum_fusion.16
  325.0 1.6 pad_maximum_fusion.28
  326.6 2.0 copy.293
  335.9 17.6 %collective-permute-done.20 = bf16[64,32,128]{2,1,0:T(8,128)(2,1)} collective-permute-done((bf16[64,32,128]{2,1,0:T(8,128)(2,1)}, bf16[64,32,128]{2,1,0:T(8,128)(2,1)}, u32[]{:S(2)}, u32[]{:S(2)}) %collective-permute-start.20) | collective-permute-done | bytes 524320 | tf_op jit(solution)/shard_map/ppermute | solution.py:68
  353.5 2.2 pad_maximum_fusion.13
  359.5 1.8 convolution_bitcast_fusion.6
  361.3 2.2 fusion.61
  365.1 2.6 fusion.30
  367.6 1.7 copy.282
  (429 shorter events, 98.4 us)
Async XLA Ops:
  0.6 13.5 %copy-start.89 = (s32[4]{0:T(128)S(1)}, s32[4]{0:T(128)}, u32[]{:S(2)}) copy-start(s32[4]{0:T(128)} %constant.134.clone) | copy-start | bytes 52
  0.6 15.5 %copy-start.88 = (s32[16]{0:T(128)S(1)}, s32[16]{0:T(128)}, u32[]{:S(2)}) copy-start(s32[16]{0:T(128)} %constant.135.clone) | copy-start | bytes 196
  0.7 10.5 %copy-start.17 = (bf16[256,2,128]{2,1,0:T(2,128)(2,1)S(1)}, bf16[256,2,128]{2,1,0:T(2,128)(2,1)}, u32[]{:S(2)}) copy-start(bf16[256,2,128]{2,1,0:T(2,128)(2,1)} %param.10) | copy-start | bytes 393220
  1.5 36.6 %copy-start.76 = (pred[32,2]{0,1:T(4,128)(4,1)}, pred[32,2]{0,1:T(4,128)(4,1)S(1)}, u32[]{:S(2)}) copy-start(pred[32,2]{0,1:T(4,128)(4,1)S(1)} %iota_compare_fusion.2) | copy-start | bytes 196
  1.5 16.2 %copy-start.87 = (s32[128]{0:T(128)S(1)}, s32[128]{0:T(128)}, u32[]{:S(2)}) copy-start(s32[128]{0:T(128)} %constant.137.clone) | copy-start | bytes 1540
  2.4 15.4 %copy-start.86 = (s32[64]{0:T(128)S(1)}, s32[64]{0:T(128)}, u32[]{:S(2)}) copy-start(s32[64]{0:T(128)} %constant.136.clone) | copy-start | bytes 772
  5.6 21.0 %copy-start.54 = (bf16[8,2,128]{2,0,1:T(8,128)(2,1)}, bf16[8,2,128]{2,0,1:T(8,128)(2,1)S(1)}, u32[]{:S(2)}) copy-start(bf16[8,2,128]{2,0,1:T(8,128)(2,1)S(1)} %get-tuple-element.25) | copy-start | bytes 12292
  5.7 33.9 %copy-start.74 = (pred[16,2]{0,1:T(4,128)(4,1)}, pred[16,2]{0,1:T(4,128)(4,1)S(1)}, u32[]{:S(2)}) copy-start(pred[16,2]{0,1:T(4,128)(4,1)S(1)} %iota_compare_fusion.1) | copy-start | bytes 100
  7.0 19.6 %copy-start.62 = (bf16[16,2,128]{2,0,1:T(8,128)(2,1)}, bf16[16,2,128]{2,0,1:T(8,128)(2,1)S(1)}, u32[]{:S(2)}) copy-start(bf16[16,2,128]{2,0,1:T(8,128)(2,1)S(1)} %get-tuple-element.24) | copy-start | bytes 24580
  7.1 34.0 %copy-start.72 = (pred[4,2]{0,1:T(4,128)(4,1)}, pred[4,2]{0,1:T(4,128)(4,1)S(1)}, u32[]{:S(2)}) copy-start(pred[4,2]{0,1:T(4,128)(4,1)S(1)} %iota_compare_fusion) | copy-start | bytes 28
  7.7 17.9 %copy-start.31 = (bf16[64,2,128]{2,0,1:T(8,128)(2,1)}, bf16[64,2,128]{2,0,1:T(8,128)(2,1)S(1)}, u32[]{:S(2)}) copy-start(bf16[64,2,128]{2,0,1:T(8,128)(2,1)S(1)} %get-tuple-element.20) | copy-start | bytes 98308
  7.7 17.9 %copy-start.33 = (bf16[64,2,128]{2,0,1:T(8,128)(2,1)}, bf16[64,2,128]{2,0,1:T(8,128)(2,1)S(1)}, u32[]{:S(2)}) copy-start(bf16[64,2,128]{2,0,1:T(8,128)(2,1)S(1)} %get-tuple-element.19) | copy-start | bytes 98308
  7.8 17.9 %copy-start.38 = (bf16[64,2,128]{2,0,1:T(8,128)(2,1)}, bf16[64,2,128]{2,0,1:T(8,128)(2,1)S(1)}, u32[]{:S(2)}) copy-start(bf16[64,2,128]{2,0,1:T(8,128)(2,1)S(1)} %get-tuple-element.21) | copy-start | bytes 98308
  8.0 17.6 %collective-permute-start = (bf16[1,1376,128]{2,1,0:T(8,128)(2,1)S(1)}, bf16[1,1376,128]{2,1,0:T(8,128)(2,1)S(1)}, u32[]{:S(2)}, u32[]{:S(2)}) collective-permute-start(bf16[1,1376,128]{2,1,0:T(8,128)(2,1)S(1)} %bitcast.330), channel_id=1, source_target_pairs={{0,8},{4,12},{8,0},{12,4},{16,24},{20,28},{24,16},{28,20},{32,40},... | collective-permute-start | bytes 1056776 | tf_op jit(solution)/shard_map/ppermute | solution.py:68
  11.2 29.1 %copy-start.40 = (bf16[256,2,128]{2,1,0:T(2,128)(2,1)S(1)}, bf16[256,2,128]{2,1,0:T(2,128)(2,1)}, u32[]{:S(2)}) copy-start(bf16[256,2,128]{2,1,0:T(2,128)(2,1)} %param.13) | copy-start | bytes 393220
  11.2 12.4 %collective-permute-start.7 = (bf16[1,688,128]{2,1,0:T(8,128)(2,1)S(1)}, bf16[1,688,128]{2,1,0:T(8,128)(2,1)S(1)}, u32[]{:S(2)}, u32[]{:S(2)}) collective-permute-start(bf16[1,688,128]{2,1,0:T(8,128)(2,1)S(1)} %maximum_bitcast_fusion), channel_id=1, source_target_pairs={{0,8},{4,12},{8,0},{12,4},{16,24},{20,28},{24,16},{28,20},{32,40},... | collective-permute-start | bytes 528392 | tf_op jit(solution)/shard_map/ppermute | solution.py:68
  23.7 6.0 %collective-permute-start.8 = (bf16[2,688,128]{2,1,0:T(8,128)(2,1)S(1)}, bf16[2,688,128]{2,1,0:T(8,128)(2,1)S(1)}, u32[]{:S(2)}, u32[]{:S(2)}) collective-permute-start(bf16[2,688,128]{2,1,0:T(8,128)(2,1)S(1)} %pad_maximum_fusion.25), channel_id=1, source_target_pairs={{0,4},{4,0},{8,12},{12,8},{16,20},{20,16},{24,28},{28,24},{32,36},... | collective-permute-start | bytes 1056776 | tf_op jit(solution)/shard_map/ppermute | solution.py:68
  26.6 21.1 %collective-permute-start.1 = (bf16[2,1376,128]{2,1,0:T(8,128)(2,1)}, bf16[2,1376,128]{2,1,0:T(8,128)(2,1)S(1)}, u32[]{:S(2)}, u32[]{:S(2)}) collective-permute-start(bf16[2,1376,128]{2,1,0:T(8,128)(2,1)} %pad_maximum_fusion.10), channel_id=1, source_target_pairs={{0,4},{4,0},{8,12},{12,8},{16,20},{20,16},{24,28},{28,24},{32,36},... | collective-permute-start | bytes 2113544 | tf_op jit(solution)/shard_map/ppermute | solution.py:68
  29.7 15.6 %collective-permute-start.11 = (bf16[4,176,128]{2,1,0:T(8,128)(2,1)S(1)}, bf16[4,176,128]{2,1,0:T(8,128)(2,1)S(1)}, u32[]{:S(2)}, u32[]{:S(2)}) collective-permute-start(bf16[4,176,128]{2,1,0:T(8,128)(2,1)S(1)} %pad_maximum_fusion.31), channel_id=1, source_target_pairs={{0,32},{4,36},{8,40},{12,44},{16,48},{20,52},{24,56},{28,60},{32,0... | collective-permute-start | bytes 540680 | tf_op jit(solution)/shard_map/ppermute | solution.py:68
  38.9 207.9 %copy-start.46 = (pred[256,2]{0,1:T(4,128)(4,1)}, pred[256,2]{0,1:T(4,128)(4,1)S(1)}, u32[]{:S(2)}) copy-start(pred[256,2]{0,1:T(4,128)(4,1)S(1)} %broadcast_in_dim.631) | copy-start | bytes 1540
  39.7 143.6 %copy-start.48 = (pred[256,2]{0,1:T(4,128)(4,1)}, pred[256,2]{0,1:T(4,128)(4,1)S(1)}, u32[]{:S(2)}) copy-start(pred[256,2]{0,1:T(4,128)(4,1)S(1)} %broadcast_in_dim.625) | copy-start | bytes 1540
  45.3 11.3 %collective-permute-start.12 = (bf16[8,176,128]{2,1,0:T(8,128)(2,1)S(1)}, bf16[8,176,128]{2,1,0:T(8,128)(2,1)S(1)}, u32[]{:S(2)}, u32[]{:S(2)}) collective-permute-start(bf16[8,176,128]{2,1,0:T(8,128)(2,1)S(1)} %pad_maximum_fusion.24), channel_id=1, source_target_pairs={{0,16},{4,20},{8,24},{12,28},{16,0},{20,4},{24,8},{28,12},{32,48},... | collective-permute-start | bytes 1081352 | tf_op jit(solution)/shard_map/ppermute | solution.py:68
  48.0 23.6 %collective-permute-start.2 = (bf16[4,352,128]{2,1,0:T(8,128)(2,1)S(1)}, bf16[4,352,128]{2,1,0:T(8,128)(2,1)S(1)}, u32[]{:S(2)}, u32[]{:S(2)}) collective-permute-start(bf16[4,352,128]{2,1,0:T(8,128)(2,1)S(1)} %pad_maximum_fusion.23), channel_id=1, source_target_pairs={{0,32},{4,36},{8,40},{12,44},{16,48},{20,52},{24,56},{28,60},{32,0... | collective-permute-start | bytes 1081352 | tf_op jit(solution)/shard_map/ppermute | solution.py:68
  57.4 20.6 %copy-start.11 = (bf16[16,48,128]{2,1,0:T(8,128)(2,1)}, bf16[16,48,128]{2,1,0:T(8,128)(2,1)S(1)}, u32[]{:S(2)}) copy-start(bf16[16,48,128]{2,1,0:T(8,128)(2,1)S(1)} %pad_maximum_fusion.30) | copy-start | bytes 589828
  57.4 10.5 %collective-permute-start.15 = (bf16[16,48,128]{2,1,0:T(8,128)(2,1)S(1)}, bf16[16,48,128]{2,1,0:T(8,128)(2,1)S(1)}, u32[]{:S(2)}, u32[]{:S(2)}) collective-permute-start(bf16[16,48,128]{2,1,0:T(8,128)(2,1)S(1)} %pad_maximum_fusion.30), channel_id=1, source_target_pairs={{0,128},{4,132},{8,136},{12,140},{16,144},{20,148},{24,152},{28,15... | collective-permute-start | bytes 589832 | tf_op jit(solution)/shard_map/ppermute | solution.py:68
  67.9 10.1 %collective-permute-start.16 = (bf16[32,48,128]{2,1,0:T(8,128)(2,1)S(1)}, bf16[32,48,128]{2,1,0:T(8,128)(2,1)S(1)}, u32[]{:S(2)}, u32[]{:S(2)}) collective-permute-start(bf16[32,48,128]{2,1,0:T(8,128)(2,1)S(1)} %pad_maximum_fusion.22), channel_id=1, source_target_pairs={{0,64},{4,68},{8,72},{12,76},{16,80},{20,84},{24,88},{28,92},{32,9... | collective-permute-start | bytes 1179656 | tf_op jit(solution)/shard_map/ppermute | solution.py:68
  71.7 17.7 %collective-permute-start.3 = (bf16[8,352,128]{2,1,0:T(8,128)(2,1)S(1)}, bf16[8,352,128]{2,1,0:T(8,128)(2,1)S(1)}, u32[]{:S(2)}, u32[]{:S(2)}) collective-permute-start(bf16[8,352,128]{2,1,0:T(8,128)(2,1)S(1)} %pad_maximum_fusion.8), channel_id=1, source_target_pairs={{0,16},{4,20},{8,24},{12,28},{16,0},{20,4},{24,8},{28,12},{32,48},... | collective-permute-start | bytes 2162696 | tf_op jit(solution)/shard_map/ppermute | solution.py:68
  78.1 11.3 %copy-start.9 = (bf16[4,352,128]{2,1,0:T(8,128)(2,1)S(1)}, bf16[4,352,128]{2,1,0:T(8,128)(2,1)}, u32[]{:S(2)}) copy-start(bf16[4,352,128]{2,1,0:T(8,128)(2,1)} %copy-done.8) | copy-start | bytes 1081348
  78.1 14.4 %copy-start.12 = (bf16[16,48,128]{2,1,0:T(8,128)(2,1)S(1)}, bf16[16,48,128]{2,1,0:T(8,128)(2,1)}, u32[]{:S(2)}) copy-start(bf16[16,48,128]{2,1,0:T(8,128)(2,1)} %copy-done.11) | copy-start | bytes 589828
  78.1 17.3 %collective-permute-start.19 = (bf16[64,16,128]{2,1,0:T(8,128)(2,1)S(1)}, bf16[64,16,128]{2,1,0:T(8,128)(2,1)S(1)}, u32[]{:S(2)}, u32[]{:S(2)}) collective-permute-start(bf16[64,16,128]{2,1,0:T(8,128)(2,1)S(1)} %pad_maximum_fusion.27), channel_id=1, source_target_pairs={{256,0},{260,4},{264,8},{268,12},{272,16},{276,20},{280,24},{284,2... | collective-permute-start | bytes 786440 | tf_op jit(solution)/shard_map/ppermute | solution.py:68
  89.4 19.1 %collective-permute-start.4 = (bf16[16,96,128]{2,1,0:T(8,128)(2,1)S(1)}, bf16[16,96,128]{2,1,0:T(8,128)(2,1)S(1)}, u32[]{:S(2)}, u32[]{:S(2)}) collective-permute-start(bf16[16,96,128]{2,1,0:T(8,128)(2,1)S(1)} %pad_maximum_fusion.20), channel_id=1, source_target_pairs={{0,128},{4,132},{8,136},{12,140},{16,144},{20,148},{24,152},{28,15... | collective-permute-start | bytes 1179656 | tf_op jit(solution)/shard_map/ppermute | solution.py:68
  97.2 18.4 %copy-start.34 = (bf16[64,2,128]{2,0,1:T(8,128)(2,1)S(1)}, bf16[64,2,128]{2,0,1:T(8,128)(2,1)}, u32[]{:S(2)}) copy-start(bf16[64,2,128]{2,0,1:T(8,128)(2,1)} %copy-done.33) | copy-start | bytes 98308
  97.2 18.4 %copy-start.37 = (pred[64,1024]{1,0:T(8,128)(4,1)S(1)}, pred[64,1024]{1,0:T(8,128)(4,1)}, u32[]{:S(2)}) copy-start(pred[64,1024]{1,0:T(8,128)(4,1)} %broadcast_compare_fusion.3) | copy-start | bytes 196612
  109.4 21.7 %collective-permute-start.5 = (bf16[32,96,128]{2,1,0:T(8,128)(2,1)}, bf16[32,96,128]{2,1,0:T(8,128)(2,1)}, u32[]{:S(2)}, u32[]{:S(2)}) collective-permute-start(bf16[32,96,128]{2,1,0:T(8,128)(2,1)} %pad_maximum_fusion.5), channel_id=1, source_target_pairs={{0,64},{4,68},{8,72},{12,76},{16,80},{20,84},{24,88},{28,92},{32,9... | collective-permute-start | bytes 2359304 | tf_op jit(solution)/shard_map/ppermute | solution.py:68
  118.9 22.9 %copy-start.4 = (bf16[16,96,128]{2,1,0:T(8,128)(2,1)S(1)}, bf16[16,96,128]{2,1,0:T(8,128)(2,1)}, u32[]{:S(2)}) copy-start(bf16[16,96,128]{2,1,0:T(8,128)(2,1)} %copy-done.3) | copy-start | bytes 1179652
  133.0 30.1 %collective-permute-start.6 = (bf16[64,32,128]{2,1,0:T(8,128)(2,1)}, bf16[64,32,128]{2,1,0:T(8,128)(2,1)}, u32[]{:S(2)}, u32[]{:S(2)}) collective-permute-start(bf16[64,32,128]{2,1,0:T(8,128)(2,1)} %pad_maximum_fusion.17), channel_id=1, source_target_pairs={{0,256},{4,260},{8,264},{12,268},{16,272},{20,276},{24,280},{28,28... | collective-permute-start | bytes 1572872 | tf_op jit(solution)/shard_map/ppermute | solution.py:68
  146.5 16.6 %copy-start.70 = (f32[16,2]{0,1:T(2,128)}, f32[16,2]{0,1:T(2,128)S(1)}, u32[]{:S(2)}) copy-start(f32[16,2]{0,1:T(2,128)S(1)} %add_bitcast_fusion.2) | copy-start | bytes 388
  167.5 15.7 %copy-start.56 = (f32[256,2]{0,1:T(2,128)}, f32[256,2]{0,1:T(2,128)S(1)}, u32[]{:S(2)}) copy-start(f32[256,2]{0,1:T(2,128)S(1)} %get-tuple-element.30) | copy-start | bytes 6148
  170.7 10.7 %copy-start.64 = (f32[16,2]{0,1:T(2,128)}, f32[16,2]{0,1:T(2,128)S(1)}, u32[]{:S(2)}) copy-start(f32[16,2]{0,1:T(2,128)S(1)} %get-tuple-element.72) | copy-start | bytes 388
  183.3 29.2 %copy-start.77 = (pred[32,2]{0,1:T(4,128)(4,1)S(1)}, pred[32,2]{0,1:T(4,128)(4,1)}, u32[]{:S(2)}) copy-start(pred[32,2]{0,1:T(4,128)(4,1)} %copy-done.76) | copy-start | bytes 196
  183.3 30.8 %copy-start.75 = (pred[16,2]{0,1:T(4,128)(4,1)S(1)}, pred[16,2]{0,1:T(4,128)(4,1)}, u32[]{:S(2)}) copy-start(pred[16,2]{0,1:T(4,128)(4,1)} %copy-done.74) | copy-start | bytes 100
  183.3 34.1 %copy-start.73 = (pred[4,2]{0,1:T(4,128)(4,1)S(1)}, pred[4,2]{0,1:T(4,128)(4,1)}, u32[]{:S(2)}) copy-start(pred[4,2]{0,1:T(4,128)(4,1)} %copy-done.72) | copy-start | bytes 28
  211.6 10.6 %copy-start.20 = (bf16[256,2,128]{0,2,1:T(8,128)(2,1)}, bf16[256,2,128]{0,2,1:T(8,128)(2,1)S(1)}, u32[]{:S(2)}) copy-start(bf16[256,2,128]{0,2,1:T(8,128)(2,1)S(1)} %get-tuple-element.29) | copy-start | bytes 393220
  226.2 24.2 %copy-start.10 = (bf16[768,128]{1,0:T(8,128)(2,1)}, bf16[768,128]{1,0:T(8,128)(2,1)S(1)}, u32[]{:S(2)}) copy-start(bf16[768,128]{1,0:T(8,128)(2,1)S(1)} %constant_dynamic-update-slice_fusion.8) | copy-start | bytes 589828
  226.3 7.6 %collective-permute-start.9 = (bf16[1,768,128]{2,1,0:T(8,128)(2,1)S(1)}, bf16[1,768,128]{2,1,0:T(8,128)(2,1)S(1)}, u32[]{:S(2)}, u32[]{:S(2)}) collective-permute-start(bf16[1,768,128]{2,1,0:T(8,128)(2,1)S(1)} %bitcast.334), channel_id=1, source_target_pairs={{0,8},{4,12},{8,0},{12,4},{16,24},{20,28},{24,16},{28,20},{32,40},... | collective-permute-start | bytes 589832 | tf_op jit(solution)/shard_map/ppermute | solution.py:68
  231.0 13.2 %copy-start.35 = (f32[64,2,128]{2,0,1:T(8,128)S(1)}, f32[64,2,128]{2,0,1:T(8,128)}, u32[]{:S(2)}) copy-start(f32[64,2,128]{2,0,1:T(8,128)} %fusion.43) | copy-start | bytes 196612
  231.0 15.8 %copy-start.21 = (bf16[256,2,128]{0,2,1:T(8,128)(2,1)S(1)}, bf16[256,2,128]{0,2,1:T(8,128)(2,1)}, u32[]{:S(2)}) copy-start(bf16[256,2,128]{0,2,1:T(8,128)(2,1)} %copy-done.20) | copy-start | bytes 393220
  231.0 15.7 %copy-start.49 = (pred[256,2]{0,1:T(4,128)(4,1)S(1)}, pred[256,2]{0,1:T(4,128)(4,1)}, u32[]{:S(2)}) copy-start(pred[256,2]{0,1:T(4,128)(4,1)} %copy-done.48) | copy-start | bytes 1540
  231.0 15.7 %copy-start.52 = (pred[256,2]{0,1:T(4,128)(4,1)S(1)}, pred[256,2]{0,1:T(4,128)(4,1)}, u32[]{:S(2)}) copy-start(pred[256,2]{0,1:T(4,128)(4,1)} %broadcast_in_dim.618) | copy-start | bytes 1540
  231.0 15.7 %copy-start.57 = (f32[256,2]{0,1:T(2,128)S(1)}, f32[256,2]{0,1:T(2,128)}, u32[]{:S(2)}) copy-start(f32[256,2]{0,1:T(2,128)} %copy-done.56) | copy-start | bytes 6148
  235.3 14.4 %collective-permute-start.10 = (bf16[2,768,128]{2,1,0:T(8,128)(2,1)}, bf16[2,768,128]{2,1,0:T(8,128)(2,1)S(1)}, u32[]{:S(2)}, u32[]{:S(2)}) collective-permute-start(bf16[2,768,128]{2,1,0:T(8,128)(2,1)} %pad_maximum_fusion.21), channel_id=1, source_target_pairs={{0,4},{4,0},{8,12},{12,8},{16,20},{20,16},{24,28},{28,24},{32,36},... | collective-permute-start | bytes 1179656 | tf_op jit(solution)/shard_map/ppermute | solution.py:68
  251.4 18.6 %collective-permute-start.13 = (bf16[4,224,128]{2,1,0:T(8,128)(2,1)S(1)}, bf16[4,224,128]{2,1,0:T(8,128)(2,1)S(1)}, u32[]{:S(2)}, u32[]{:S(2)}) collective-permute-start(bf16[4,224,128]{2,1,0:T(8,128)(2,1)S(1)} %pad_maximum_fusion.29), channel_id=1, source_target_pairs={{0,32},{4,36},{8,40},{12,44},{16,48},{20,52},{24,56},{28,60},{32,0... | collective-permute-start | bytes 688136 | tf_op jit(solution)/shard_map/ppermute | solution.py:68
  255.5 17.5 %copy-start.19 = (bf16[256,2,128]{2,1,0:T(2,128)(2,1)S(1)}, bf16[256,2,128]{2,1,0:T(2,128)(2,1)}, u32[]{:S(2)}) copy-start(bf16[256,2,128]{2,1,0:T(2,128)(2,1)} %param.11) | copy-start | bytes 393220
  270.0 15.8 %collective-permute-start.14 = (bf16[8,224,128]{2,1,0:T(8,128)(2,1)S(1)}, bf16[8,224,128]{2,1,0:T(8,128)(2,1)S(1)}, u32[]{:S(2)}, u32[]{:S(2)}) collective-permute-start(bf16[8,224,128]{2,1,0:T(8,128)(2,1)S(1)} %pad_maximum_fusion.19), channel_id=1, source_target_pairs={{0,16},{4,20},{8,24},{12,28},{16,0},{20,4},{24,8},{28,12},{32,48},... | collective-permute-start | bytes 1376264 | tf_op jit(solution)/shard_map/ppermute | solution.py:68
  285.9 15.5 %collective-permute-start.17 = (bf16[16,80,128]{2,1,0:T(8,128)(2,1)S(1)}, bf16[16,80,128]{2,1,0:T(8,128)(2,1)}, u32[]{:S(2)}, u32[]{:S(2)}) collective-permute-start(bf16[16,80,128]{2,1,0:T(8,128)(2,1)S(1)} %pad_maximum_fusion.26), channel_id=1, source_target_pairs={{0,128},{4,132},{8,136},{12,140},{16,144},{20,148},{24,152},{28,15... | collective-permute-start | bytes 983048 | tf_op jit(solution)/shard_map/ppermute | solution.py:68
  289.4 18.0 %copy-start.39 = (bf16[64,2,128]{2,0,1:T(8,128)(2,1)S(1)}, bf16[64,2,128]{2,0,1:T(8,128)(2,1)}, u32[]{:S(2)}) copy-start(bf16[64,2,128]{2,0,1:T(8,128)(2,1)} %copy-done.38) | copy-start | bytes 98308
  290.5 19.1 %copy-start.32 = (bf16[64,2,128]{2,0,1:T(8,128)(2,1)S(1)}, bf16[64,2,128]{2,0,1:T(8,128)(2,1)}, u32[]{:S(2)}) copy-start(bf16[64,2,128]{2,0,1:T(8,128)(2,1)} %copy-done.31) | copy-start | bytes 98308
  291.3 18.4 %copy-start.58 = (f32[2,1024]{1,0:T(2,128)S(1)}, f32[2,1024]{1,0:T(2,128)}, u32[]{:S(2)}) copy-start(f32[2,1024]{1,0:T(2,128)} %sub.438) | copy-start | bytes 24580
  303.3 18.2 %collective-permute-start.18 = (bf16[32,80,128]{2,1,0:T(8,128)(2,1)}, bf16[32,80,128]{2,1,0:T(8,128)(2,1)}, u32[]{:S(2)}, u32[]{:S(2)}) collective-permute-start(bf16[32,80,128]{2,1,0:T(8,128)(2,1)} %pad_maximum_fusion.12), channel_id=1, source_target_pairs={{0,64},{4,68},{8,72},{12,76},{16,80},{20,84},{24,88},{28,92},{32,9... | collective-permute-start | bytes 1966088 | tf_op jit(solution)/shard_map/ppermute | solution.py:68
  317.5 12.2 %copy-start.63 = (bf16[16,2,128]{2,0,1:T(8,128)(2,1)S(1)}, bf16[16,2,128]{2,0,1:T(8,128)(2,1)}, u32[]{:S(2)}) copy-start(bf16[16,2,128]{2,0,1:T(8,128)(2,1)} %copy-done.62) | copy-start | bytes 24580
  317.5 12.2 %copy-start.71 = (pred[1024,16]{0,1:T(8,128)(4,1)S(1)}, pred[1024,16]{0,1:T(8,128)(4,1)}, u32[]{:S(2)}) copy-start(pred[1024,16]{0,1:T(8,128)(4,1)} %broadcast_compare_fusion.4) | copy-start | bytes 49156
  323.6 29.9 %collective-permute-start.20 = (bf16[64,32,128]{2,1,0:T(8,128)(2,1)}, bf16[64,32,128]{2,1,0:T(8,128)(2,1)}, u32[]{:S(2)}, u32[]{:S(2)}) collective-permute-start(bf16[64,32,128]{2,1,0:T(8,128)(2,1)} %get-tuple-element.33), channel_id=1, source_target_pairs={{256,0},{260,4},{264,8},{268,12},{272,16},{276,20},{280,24},{284,2... | collective-permute-start | bytes 1572872 | tf_op jit(solution)/shard_map/ppermute | solution.py:68
  335.9 22.3 %copy-start.69 = (bf16[8,2,128]{2,0,1:T(8,128)(2,1)S(1)}, bf16[8,2,128]{2,0,1:T(8,128)(2,1)}, u32[]{:S(2)}) copy-start(bf16[8,2,128]{2,0,1:T(8,128)(2,1)} %copy-done.68) | copy-start | bytes 12292
  335.9 22.3 %copy-start.80 = (pred[1024,8]{0,1:T(8,128)(4,1)S(1)}, pred[1024,8]{0,1:T(8,128)(4,1)}, u32[]{:S(2)}) copy-start(pred[1024,8]{0,1:T(8,128)(4,1)} %broadcast_compare_fusion.6) | copy-start | bytes 24580
  (47 other events, 212.3 us)
